TPU v7x, 32 devices: a whole 2x2x4 slice. The times are simulated.
32 devices in a mesh: groups: 2 (over y), tm: 16 (over z, x, core).
Axes of the slice: x: 2, y: 2, z: 4, core: 2. Of those that a mesh axis runs over, the one named last changes fastest.
Arguments:
- ref_traj: float32 [8, 1024, 256], P('groups', 'tm'), parts along dimension 0, may hold values from -6 to 6
- cost_weights: float32 [8, 1024, 256], P('groups', 'tm'), parts along dimension 0, may hold values from 0.1 to 10
- x_init: float32 [8, 256], P('groups'), parts along dimension 0, may hold values from -6 to 6
- decay: float32 [256], replicated, as said below
- coupling: float32 [3, 64, 64], replicated, may hold values from -0.00018310547 to 0.00018310547
- links: int32 [3, 2], replicated, may hold values from 0 to 3, as said below
- input_map: float32 [256, 64], replicated, may hold values from -0.0007324219 to 0.0007324219
- ff_gain: float32 [64, 256], replicated, may hold values from -0.01171875 to 0.01171875
- lengths: int32 [8, 4], P('groups'), parts along dimension 0, may hold values from 1 to 512, 1024 in all within a row
Outputs:
- states: float32 [8, 1024, 256], P('groups', 'tm'), parts along dimension 0
- weight_grad: float32 [8, 1024, 256], P('groups', 'tm'), parts along dimension 0
- cost: float32 [8], P('groups'), parts along dimension 0
There are 2 independent parts, one for each index of `groups`. A program takes and returns all parts, laid end to end along the dimension named above; an argument that names none is the same for every part. Nothing has to cross between parts.
Inputs may be any that keep to these rules, and one draw needn't show every extreme that they name: `links`: each pair names two different blocks, the row before the column, and no pair twice. The lengths of a scenario sum to 1024, and the longest is exactly 512. `decay`: every entry lies strictly between 0 and 1.
All inputs are finite; a program needn't handle non-finite values.
Results may differ from a plain program's by a relative error of at most 0.0003.
Values sent between devices are 32-bit elements; how exact they have to be, the bound alone decides.
No kernel may reach another device: no remote copies, remote signals or barrier semaphores. Data moves between devices by JAX's collectives and lax.ppermute only.
A program may use at most 64 MiB of HBM per device.

v0:
```python
import jax
import jax.numpy as jnp
from jax import lax
from jax.sharding import PartitionSpec as P


def build_dynamics(decay, coupling, links):
    size = decay.shape[0]
    width = coupling.shape[1]
    lanes = jnp.arange(size, dtype=jnp.int32)
    offsets = jnp.arange(width, dtype=jnp.int32)
    row_hot = (lanes[None, :, None] == links[:, 0:1, None] * width + offsets[None, None, :]).astype(
        jnp.float32
    )
    col_hot = (lanes[None, :, None] == links[:, 1:2, None] * width + offsets[None, None, :]).astype(
        jnp.float32
    )
    placed = jnp.einsum(
        "lia,lab,ljb->ij", row_hot, coupling, col_hot, precision=lax.Precision.HIGHEST
    )
    return jnp.diag(decay) + placed


def row_times(values, matrix):
    width = values.shape[-1]
    flat = jnp.dot(values.reshape(-1, width), matrix, precision=lax.Precision.HIGHEST)
    return flat.reshape(values.shape)


def run_chain(inputs, frame_starts, powers, backward, local_levels, device_levels):
    scen_count, seg_steps, width = inputs.shape
    devices = lax.axis_size("tm")
    device = lax.axis_index("tm")
    if backward:
        driven = inputs[:, ::-1]
        frame_device = devices - 1 - device
    else:
        driven = inputs
        frame_device = device
    positions = frame_device * seg_steps + jnp.arange(seg_steps, dtype=jnp.int32)
    cut_here = jnp.any(positions[None, :, None] == frame_starts[:, None, :], axis=-1)
    values = driven
    flags = 1.0 - cut_here.astype(jnp.float32)
    for level in range(local_levels):
        stride = 2**level
        prior_values = jnp.pad(values[:, : seg_steps - stride], ((0, 0), (stride, 0), (0, 0)))
        prior_flags = jnp.pad(
            flags[:, : seg_steps - stride], ((0, 0), (stride, 0)), constant_values=1.0
        )
        values = values + flags[:, :, None] * row_times(prior_values, powers[level])
        flags = flags * prior_flags
    last_value = values[:, -1]
    last_flag = flags[:, -1]
    all_values, all_flags = (
        lax.all_gather(last_value[None], "tm", axis=0, tiled=True),
        lax.all_gather(last_flag[None], "tm", axis=0, tiled=True),
    )
    if backward:
        all_values = all_values[::-1]
        all_flags = all_flags[::-1]
    roll_by = devices - frame_device
    all_values = jnp.roll(all_values, roll_by, axis=0)
    all_flags = jnp.roll(all_flags, roll_by, axis=0)
    keep = (jnp.arange(devices, dtype=jnp.int32) >= roll_by).astype(jnp.float32)
    all_values = all_values * keep[:, None, None]
    all_flags = all_flags * keep[:, None] + (1.0 - keep[:, None])
    for level in range(device_levels):
        half = all_values.shape[0] // 2
        paired_values = all_values.reshape(half, 2, scen_count, width)
        paired_flags = all_flags.reshape(half, 2, scen_count)
        moved = row_times(paired_values[:, 0], powers[local_levels + level])
        all_values = paired_flags[:, 1, :, None] * moved + paired_values[:, 1]
        all_flags = paired_flags[:, 0] * paired_flags[:, 1]
    entering = all_values[0]
    table = row_times(entering[:, None, :], powers[0])
    for level in range(local_levels):
        table = jnp.concatenate([table, row_times(table, powers[level])], axis=1)
    result = values + flags[:, :, None] * table
    if backward:
        result = result[:, ::-1]
    return result


def per_device(ref_traj, cost_weights, x_init, decay, coupling, links, input_map, ff_gain, lengths):
    scen_count, seg_steps, width = ref_traj.shape
    devices = lax.axis_size("tm")
    device = lax.axis_index("tm")
    total = seg_steps * devices
    high = lax.Precision.HIGHEST
    dynamics = build_dynamics(decay, coupling, links)
    local_levels = seg_steps.bit_length() - 1
    device_levels = (devices - 1).bit_length()
    power_count = local_levels + max(device_levels, 1)
    squares = [dynamics]
    for level in range(power_count - 1):
        squares.append(jnp.dot(squares[-1], squares[-1], precision=high))
    forward_powers = [matrix.T for matrix in squares]
    ends_incl = jnp.cumsum(lengths, axis=1)
    starts = ends_incl - lengths
    mirrored = total - ends_incl
    value_term = run_chain(
        cost_weights * ref_traj, mirrored, squares, True, local_levels, device_levels
    )
    controls = jnp.einsum("stn,cn->stc", value_term, ff_gain, precision=high)
    forcing = -jnp.einsum("stc,nc->stn", controls, input_map, precision=high)
    positions = device * seg_steps + jnp.arange(seg_steps, dtype=jnp.int32)
    start_flag = jnp.any(positions[None, :, None] == starts[:, None, :], axis=-1).astype(
        jnp.float32
    )
    init_image = jnp.dot(x_init, dynamics.T, precision=high)
    driven = forcing + start_flag[:, :, None] * init_image[:, None, :]
    states = run_chain(driven, starts, forward_powers, False, local_levels, device_levels)
    offset = states - ref_traj
    local_cost = jnp.sum(cost_weights * offset * offset, axis=(1, 2)) * (0.5 / total)
    cost = lax.psum(local_cost, "tm")
    adjoint = run_chain(cost_weights * offset, mirrored, squares, True, local_levels, device_levels)
    pulled = jnp.einsum("stn,nc->stc", adjoint, input_map, precision=high)
    source = -jnp.einsum("stc,cn->stn", pulled, ff_gain, precision=high)
    value_adjoint = run_chain(source, starts, forward_powers, False, local_levels, device_levels)
    weight_grad = 0.5 * offset * offset + ref_traj * value_adjoint
    return (states, weight_grad, cost)


def solution(mesh):
    placed = (
        P("groups", "tm", None),
        P("groups", "tm", None),
        P("groups", None),
        P(),
        P(),
        P(),
        P(),
        P(),
        P("groups", None),
    )
    return jax.shard_map(
        per_device,
        mesh=mesh,
        in_specs=placed,
        out_specs=(P("groups", "tm", None), P("groups", "tm", None), P("groups")),
        check_vma=False,
    )
```

profile of v0, /device:TPU:0, one launch (start us, length us, event | category | flops | bytes accessed | tf_op | source)
XLA Modules:
  0.0 228.4 jit_solution(11940536303902532036)
XLA Ops:
  0.7 0.6 copy-done.79
  2.7 0.7 copy-done.78
  3.3 0.7 copy-done.66
  9.9 34.9 %all-reduce.38 = (f32[64]{0:T(128)S(1)}, f32[64]{0:T(128)S(1)}) all-reduce(f32[64]{0:T(128)S(1)} %dynamic-update-slice, f32[64]{0:T(128)S(1)} %dynamic-update-slice.1), channel_id=2, replica_groups=mesh['groups'=2,'tm'=16] {'tm'}, use_global_device_ids=true, to_apply=%add.36 | all-reduce | flops 128 | bytes 1024
  47.5 0.7 copy.317
  49.6 0.9 convolution_bitcast_fusion.2
  54.7 0.8 rev.22
  55.4 0.8 slice.317
  56.4 1.3 fusion.23
  59.8 17.5 %all-gather.1 = f32[64,1,256]{2,1,0:T(1,128)S(1)} all-gather(f32[4,1,256]{2,1,0:T(1,128)S(1)} %slice.420), channel_id=3, replica_groups=mesh['groups'=2,'tm'=16] {'tm'}, dimensions={0}, use_global_device_ids=true | all-gather | bytes 69632 | tf_op jit(solution)/shard_map/all_gather | solution.py:55
  81.0 0.9 fusion.68
  81.9 2.5 %concatenate.103 = f32[4,64,256]{2,1,0:T(8,128)S(1)} concatenate(f32[4,1,256]{2,1,0:T(1,128)} %copy-done.14, f32[4,1,256]{2,1,0:T(1,128)} %copy-done.16, f32[4,2,256]{2,1,0:T(2,128)} %copy-done.12, f32[4,4,256]{2,1,0:T(4,128)S(1)} %fusion.104, f32[4,8,256]{2,1,0:T(8,128)S(1)} %fusion.92, f32[4,16,256]{2,1,0:T(8,128)} %copy-done.6, f32[4,32,256]{2,1,0:T(8,128)} %fusion.68), dimensions={1} | concatenate | bytes 524288 | tf_op jit(solution)/shard_map/concatenate | solution.py:77
  84.4 1.5 multiply_add_fusion.2
  85.9 1.0 rev.25
  90.2 0.6 copy-done.25
  91.3 0.6 copy-done.22
  92.4 0.6 copy-done.19
  93.5 19.2 %all-gather.3 = f32[64,1,256]{2,1,0:T(1,128)S(1)} all-gather(f32[4,1,256]{2,1,0:T(1,128)S(1)} %slice.441), channel_id=5, replica_groups=mesh['groups'=2,'tm'=16] {'tm'}, dimensions={0}, use_global_device_ids=true | all-gather | bytes 69632 | tf_op jit(solution)/shard_map/all_gather | solution.py:55
  113.6 0.7 copy-done.52
  114.7 0.7 copy-done.56
  115.7 0.6 copy-done.61
  119.4 1.1 fusion.65
  120.5 3.5 %concatenate.109 = f32[4,64,256]{2,1,0:T(8,128)} concatenate(f32[4,1,256]{2,1,0:T(1,128)S(1)} %reshape.528, f32[4,1,256]{2,1,0:T(1,128)S(1)} %reshape.529, f32[4,2,256]{2,1,0:T(2,128)S(1)} %copy.331, f32[4,4,256]{2,1,0:T(4,128)S(1)} %fusion.101, f32[4,8,256]{2,1,0:T(8,128)S(1)} %fusion.89, f32[4,16,256]{2,1,0:T(8,128)S(1)} %fusion.77, f32[4,32,256]{2,1,0:T(8,128)} %fusion.65), dimensions={1} | concatenate | bytes 524288 | tf_op jit(solution)/shard_map/concatenate | solution.py:77
  124.0 1.9 multiply_reduce_fusion
  125.9 30.3 %psum.7 = f32[4]{0:T(128)} all-reduce(f32[4]{0:T(128)S(1)} %broadcast_multiply_fusion), channel_id=1, replica_groups=mesh['groups'=2,'tm'=16] {'tm'}, use_global_device_ids=true, to_apply=%region_4.7 | all-reduce | flops 4 | bytes 32 | tf_op jit(solution)/shard_map/psum | solution.py:115
  156.3 0.8 rev.26
  157.0 0.8 slice.378
  158.0 1.3 fusion.11
  161.5 0.7 copy-done.36
  162.5 0.7 copy-done.34
  163.6 17.5 %all-gather.4 = f32[64,1,256]{2,1,0:T(1,128)S(1)} all-gather(f32[4,1,256]{2,1,0:T(1,128)S(1)} %slice.456), channel_id=6, replica_groups=mesh['groups'=2,'tm'=16] {'tm'}, dimensions={0}, use_global_device_ids=true | all-gather | bytes 69632 | tf_op jit(solution)/shard_map/all_gather | solution.py:55
  181.3 0.6 copy-done.71
  182.1 0.7 copy-done.55
  183.1 0.7 copy-done.59
  184.0 0.7 copy-done.64
  187.8 0.9 fusion.62
  188.7 2.5 %concatenate.115 = f32[4,64,256]{2,1,0:T(8,128)S(1)} concatenate(f32[4,1,256]{2,1,0:T(1,128)} %copy-done.15, f32[4,1,256]{2,1,0:T(1,128)} %copy-done.17, f32[4,2,256]{2,1,0:T(2,128)} %copy-done.13, f32[4,4,256]{2,1,0:T(4,128)S(1)} %fusion.98, f32[4,8,256]{2,1,0:T(8,128)S(1)} %fusion.86, f32[4,16,256]{2,1,0:T(8,128)} %copy-done.7, f32[4,32,256]{2,1,0:T(8,128)} %fusion.62), dimensions={1} | concatenate | bytes 524288 | tf_op jit(solution)/shard_map/concatenate | solution.py:77
  191.2 1.5 multiply_add_fusion
  192.7 1.0 rev.28
  197.0 0.6 copy-done.26
  198.1 0.6 copy-done.23
  199.2 0.6 copy-done.20
  200.3 19.2 %all-gather.5 = f32[64,1,256]{2,1,0:T(1,128)S(1)} all-gather(f32[4,1,256]{2,1,0:T(1,128)S(1)} %slice.471), channel_id=7, replica_groups=mesh['groups'=2,'tm'=16] {'tm'}, dimensions={0}, use_global_device_ids=true | all-gather | bytes 69632 | tf_op jit(solution)/shard_map/all_gather | solution.py:55
  220.4 0.7 copy-done.53
  221.5 0.7 copy-done.57
  222.5 0.6 copy-done.62
  226.7 0.9 copy-done.3
  227.6 0.8 fusion.46
  (344 shorter events, 45.6 us)
Async XLA Ops:
  0.6 47.6 %copy-start = (f32[3,64,64]{2,1,0:T(8,128)S(1)}, f32[3,64,64]{2,1,0:T(8,128)}, u32[]{:S(2)}) copy-start(f32[3,64,64]{2,1,0:T(8,128)} %param.17) | copy-start | bytes 147460
  2.6 74.9 %copy-start.70 = (f32[16]{0:T(128)}, f32[16]{0:T(128)S(1)}, u32[]{:S(2)}) copy-start(f32[16]{0:T(128)S(1)} %compare_convert_fusion.1) | copy-start | bytes 196
  2.6 43.0 %copy-start.67 = (f32[16]{0:T(128)}, f32[16]{0:T(128)S(1)}, u32[]{:S(2)}) copy-start(f32[16]{0:T(128)S(1)} %compare_convert_fusion) | copy-start | bytes 196
  2.7 0.7 copy-start.78
  3.3 0.7 copy-start.66
  4.3 51.9 %copy-start.50 = (f32[4,64]{1,0:T(4,128)}, f32[4,64]{1,0:T(4,128)S(1)}, u32[]{:S(2)}) copy-start(f32[4,64]{1,0:T(4,128)S(1)} %convert_subtract_fusion) | copy-start | bytes 3076
  4.4 53.3 %copy-start.41 = (f32[4,64]{1,0:T(4,128)}, f32[4,64]{1,0:T(4,128)S(1)}, u32[]{:S(2)}) copy-start(f32[4,64]{1,0:T(4,128)S(1)} %pad_multiply_fusion.11) | copy-start | bytes 3076
  4.5 53.7 %copy-start.39 = (f32[4,64]{1,0:T(4,128)}, f32[4,64]{1,0:T(4,128)S(1)}, u32[]{:S(2)}) copy-start(f32[4,64]{1,0:T(4,128)S(1)} %pad_multiply_fusion.10) | copy-start | bytes 3076
  4.6 54.0 %copy-start.37 = (f32[4,64]{1,0:T(4,128)}, f32[4,64]{1,0:T(4,128)S(1)}, u32[]{:S(2)}) copy-start(f32[4,64]{1,0:T(4,128)S(1)} %pad_multiply_fusion.9) | copy-start | bytes 3076
  4.6 54.4 %copy-start.35 = (f32[4,64]{1,0:T(4,128)}, f32[4,64]{1,0:T(4,128)S(1)}, u32[]{:S(2)}) copy-start(f32[4,64]{1,0:T(4,128)S(1)} %pad_multiply_fusion.8) | copy-start | bytes 3076
  4.7 54.7 %copy-start.33 = (f32[4,64]{1,0:T(4,128)}, f32[4,64]{1,0:T(4,128)S(1)}, u32[]{:S(2)}) copy-start(f32[4,64]{1,0:T(4,128)S(1)} %pad_multiply_fusion.7) | copy-start | bytes 3076
  45.3 32.7 %copy-start.58 = (f32[4,1,4]{2,1,0:T(1,128)}, f32[4,1,4]{2,1,0:T(1,128)S(1)}, u32[]{:S(2)}) copy-start(f32[4,1,4]{2,1,0:T(1,128)S(1)} %get-tuple-element.34) | copy-start | bytes 196
  45.3 32.9 %copy-start.63 = (f32[2,1,4]{2,1,0:T(1,128)}, f32[2,1,4]{2,1,0:T(1,128)S(1)}, u32[]{:S(2)}) copy-start(f32[2,1,4]{2,1,0:T(1,128)S(1)} %get-tuple-element.38) | copy-start | bytes 100
  45.3 33.1 %copy-start.75 = (f32[4]{0:T(128)}, f32[4]{0:T(128)S(1)}, u32[]{:S(2)}) copy-start(f32[4]{0:T(128)S(1)} %slice_bitcast_fusion.25) | copy-start | bytes 52
  45.4 32.2 %copy-start.54 = (f32[8,1,4]{0,2,1:T(4,128)}, f32[8,1,4]{0,2,1:T(4,128)S(1)}, u32[]{:S(2)}) copy-start(f32[8,1,4]{0,2,1:T(4,128)S(1)} %copy.299) | copy-start | bytes 388
  48.2 0.7 copy-start.77
  48.9 0.7 copy-start.72
  53.6 1.0 copy-start.1
  53.6 1.0 copy-start.2
  55.4 0.9 copy-start.5
  79.0 1.4 copy-start.14
  79.2 1.1 copy-start.16
  79.5 0.8 copy-start.12
  85.9 1.0 copy-start.10
  86.9 0.8 copy-start.8
  86.9 0.8 copy-start.60
  87.0 0.8 copy-start.65
  89.1 0.7 copy-start.31
  90.2 0.7 copy-start.25
  113.6 0.7 copy-start.52
  120.5 3.5 %copy-start.44 = (f32[4,64]{1,0:T(4,128)S(1)}, f32[4,64]{1,0:T(4,128)}, u32[]{:S(2)}) copy-start(f32[4,64]{1,0:T(4,128)} %copy-done.43) | copy-start | bytes 3076
  157.0 0.9 copy-start.4
  157.0 1.0 copy-start.51
  158.0 1.4 copy-start.42
  161.4 0.7 copy-start.36
  162.5 0.7 copy-start.34
  182.1 0.7 copy-start.55
  185.7 1.4 copy-start.15
  186.0 1.1 copy-start.17
  186.3 0.8 copy-start.13
  192.7 1.0 copy-start.9
  193.7 0.8 copy-start.11
  195.9 0.7 copy-start.32
  197.0 0.7 copy-start.26
  198.1 0.7 copy-start.23
  220.3 0.7 copy-start.53
  226.6 1.0 copy-start.3
  226.6 0.9 copy-start.45
  (32 other events, 20.2 us)
where the time goes:
time: 230 us; the launch traced here: 228 us
  blocking collectives  139 us (60%)
  local copies, waits for them, and re-layouts  44.1 us (19%)
  matrix products  32.4 us (14%)
  other arithmetic  10.2 us (4%)
  between operations  3.01 us (1%)
    all_gather x4, blocking collectives, run_chain(): lax.all_gather(last_value[None], 'tm', axis=0, tiled=True)  73.5 us
    unnamed x1, blocking collectives  34.9 us
    psum x1, blocking collectives, per_device(): cost = lax.psum(local_cost, 'tm')  30.3 us
    unnamed x165, local copies, waits for them, and re-layouts  27.1 us
    dot_general x68, matrix products, row_times(): jnp.dot(values.reshape(-1, width), matrix, precision=lax.Precision.HIGHEST)  25.8 us
    concatenate x12, local copies, waits for them, and re-layouts, run_chain(): table = jnp.concatenate([table, row_times(table, powers[level])], axis=1)  8.84 us

commit v1 on v0

--- a/solution.py
+++ b/solution.py
@@ -2,6 +2,7 @@
 import jax.numpy as jnp
 from jax import lax
 from jax.sharding import PartitionSpec as P
+from jax.lax import axis_index, axis_size, ppermute
 
 
 def build_dynamics(decay, coupling, links):
@@ -51,8 +52,23 @@
         flags = flags * prior_flags
     last_value = values[:, -1]
     last_flag = flags[:, -1]
+
+    def draft_stocks(panel, axis_key):
+        inter = axis_size(axis_key)
+        value_now = axis_index(axis_key)
+        part_now, big, mat_out = (inter, value_now, panel.shape[0])
+        sides = [(w, (w + 1) % part_now) for w in range(part_now)]
+        plain = jnp.zeros((*panel.shape[:0], part_now * mat_out, *panel.shape[1:]), panel.dtype)
+        a_now = panel
+        for dev_i in range(part_now):
+            r_now = (big - dev_i) % part_now
+            plain = lax.dynamic_update_slice_in_dim(plain, a_now, r_now * mat_out, axis=0)
+            if dev_i < part_now - 1:
+                a_now = ppermute(a_now, axis_key, sides)
+        return plain
+
     all_values, all_flags = (
-        lax.all_gather(last_value[None], "tm", axis=0, tiled=True),
+        draft_stocks(last_value[None], "tm"),
         lax.all_gather(last_flag[None], "tm", axis=0, tiled=True),
     )
     if backward:

time: 230 us -> 479 us (2.08)
  waiting for transfers between devices: 0 us -> 332 us
  blocking collectives: 139 us -> 69.1 us
  local copies, waits for them, and re-layouts: 44.1 us -> 33.5 us
    ppermute x0 -> x60, waiting for transfers between devices: none -> 332 us  [draft_stocks(): a_now = ppermute(a_now, axis_key, sides)]
    all_gather x4 -> x0, blocking collectives: 73.5 us -> none  [run_chain(): lax.all_gather(last_value[None], 'tm', axis=0, tiled=True)]
    unnamed x165 -> x129, local copies, waits for them, and re-layouts: 27.1 us -> 20.7 us
  transfers between devices with their start and end apart: 0 -> 60, of which waited for: 0 -> 58; matrix products, arithmetic and copies ran while one was open for 0% -> 2% of each run, Pallas kernels for 0% -> 0%
where the time goes in v1:
time: 479 us; the launch traced here: 478 us
  waiting for transfers between devices  332 us (69%)
  blocking collectives  69.1 us (14%)
  local copies, waits for them, and re-layouts  33.5 us (7%)
  matrix products  30.9 us (6%)
  other arithmetic  9.27 us (2%)
    ppermute x60, waiting for transfers between devices, draft_stocks(): a_now = ppermute(a_now, axis_key, sides)  332 us
    unnamed x1, blocking collectives  34.7 us
    psum x1, blocking collectives, per_device(): cost = lax.psum(local_cost, 'tm')  34.4 us
    dot_general x68, matrix products, row_times(): jnp.dot(values.reshape(-1, width), matrix, precision=lax.Precision.HIGHEST)  24.4 us
    unnamed x129, local copies, waits for them, and re-layouts  20.7 us
  transfers between devices with their start and end apart: 60, of which 58 were waited for; matrix products, arithmetic and copies ran while one was open for 2% of the time, Pallas kernels for 0%

profile of v1, /device:TPU:0, one launch (start us, length us, event | category | flops | bytes accessed | tf_op | source)
XLA Modules:
  0.0 478.2 jit_solution(10078735134394712403)
XLA Ops:
  17.1 34.7 %all-reduce.38 = (f32[64]{0:T(128)S(1)}, f32[64]{0:T(128)S(1)}) all-reduce(f32[64]{0:T(128)S(1)} %dynamic-update-slice, f32[64]{0:T(128)S(1)} %dynamic-update-slice.1), channel_id=2, replica_groups=mesh['groups'=2,'tm'=16] {'tm'}, use_global_device_ids=true, to_apply=%add.36 | all-reduce | flops 128 | bytes 1024
  58.3 5.7 %collective-permute-done.1 = f32[1,4,256]{2,0,1:T(1,128)S(1)} collective-permute-done((f32[1,4,256]{2,0,1:T(1,128)S(1)}, f32[1,4,256]{2,0,1:T(1,128)S(1)}, u32[]{:S(2)}, u32[]{:S(2)}) %collective-permute-start.1) | collective-permute-done | bytes 4128 | tf_op jit(solution)/shard_map/ppermute | solution.py:67
  64.0 5.7 %collective-permute-done.2 = f32[1,4,256]{2,0,1:T(1,128)S(1)} collective-permute-done((f32[1,4,256]{2,0,1:T(1,128)S(1)}, f32[1,4,256]{2,0,1:T(1,128)S(1)}, u32[]{:S(2)}, u32[]{:S(2)}) %collective-permute-start.2) | collective-permute-done | bytes 4128 | tf_op jit(solution)/shard_map/ppermute | solution.py:67
  69.7 5.7 %collective-permute-done.3 = f32[1,4,256]{2,0,1:T(1,128)S(1)} collective-permute-done((f32[1,4,256]{2,0,1:T(1,128)S(1)}, f32[1,4,256]{2,0,1:T(1,128)S(1)}, u32[]{:S(2)}, u32[]{:S(2)}) %collective-permute-start.3) | collective-permute-done | bytes 4128 | tf_op jit(solution)/shard_map/ppermute | solution.py:67
  75.5 5.7 %collective-permute-done.4 = f32[1,4,256]{2,0,1:T(1,128)S(1)} collective-permute-done((f32[1,4,256]{2,0,1:T(1,128)S(1)}, f32[1,4,256]{2,0,1:T(1,128)S(1)}, u32[]{:S(2)}, u32[]{:S(2)}) %collective-permute-start.4) | collective-permute-done | bytes 4128 | tf_op jit(solution)/shard_map/ppermute | solution.py:67
  81.2 5.7 %collective-permute-done.5 = f32[1,4,256]{2,0,1:T(1,128)S(1)} collective-permute-done((f32[1,4,256]{2,0,1:T(1,128)S(1)}, f32[1,4,256]{2,0,1:T(1,128)S(1)}, u32[]{:S(2)}, u32[]{:S(2)}) %collective-permute-start.5) | collective-permute-done | bytes 4128 | tf_op jit(solution)/shard_map/ppermute | solution.py:67
  86.9 5.7 %collective-permute-done.6 = f32[1,4,256]{2,0,1:T(1,128)S(1)} collective-permute-done((f32[1,4,256]{2,0,1:T(1,128)S(1)}, f32[1,4,256]{2,0,1:T(1,128)S(1)}, u32[]{:S(2)}, u32[]{:S(2)}) %collective-permute-start.6) | collective-permute-done | bytes 4128 | tf_op jit(solution)/shard_map/ppermute | solution.py:67
  92.7 5.7 %collective-permute-done.7 = f32[1,4,256]{2,0,1:T(1,128)S(1)} collective-permute-done((f32[1,4,256]{2,0,1:T(1,128)S(1)}, f32[1,4,256]{2,0,1:T(1,128)S(1)}, u32[]{:S(2)}, u32[]{:S(2)}) %collective-permute-start.7) | collective-permute-done | bytes 4128 | tf_op jit(solution)/shard_map/ppermute | solution.py:67
  98.4 5.7 %collective-permute-done.8 = f32[1,4,256]{2,0,1:T(1,128)S(1)} collective-permute-done((f32[1,4,256]{2,0,1:T(1,128)S(1)}, f32[1,4,256]{2,0,1:T(1,128)S(1)}, u32[]{:S(2)}, u32[]{:S(2)}) %collective-permute-start.8) | collective-permute-done | bytes 4128 | tf_op jit(solution)/shard_map/ppermute | solution.py:67
  104.1 5.7 %collective-permute-done.9 = f32[1,4,256]{2,0,1:T(1,128)S(1)} collective-permute-done((f32[1,4,256]{2,0,1:T(1,128)S(1)}, f32[1,4,256]{2,0,1:T(1,128)S(1)}, u32[]{:S(2)}, u32[]{:S(2)}) %collective-permute-start.9) | collective-permute-done | bytes 4128 | tf_op jit(solution)/shard_map/ppermute | solution.py:67
  109.9 5.7 %collective-permute-done.10 = f32[1,4,256]{2,0,1:T(1,128)S(1)} collective-permute-done((f32[1,4,256]{2,0,1:T(1,128)S(1)}, f32[1,4,256]{2,0,1:T(1,128)S(1)}, u32[]{:S(2)}, u32[]{:S(2)}) %collective-permute-start.10) | collective-permute-done | bytes 4128 | tf_op jit(solution)/shard_map/ppermute | solution.py:67
  115.6 5.7 %collective-permute-done.11 = f32[1,4,256]{2,0,1:T(1,128)S(1)} collective-permute-done((f32[1,4,256]{2,0,1:T(1,128)S(1)}, f32[1,4,256]{2,0,1:T(1,128)S(1)}, u32[]{:S(2)}, u32[]{:S(2)}) %collective-permute-start.11) | collective-permute-done | bytes 4128 | tf_op jit(solution)/shard_map/ppermute | solution.py:67
  121.3 5.7 %collective-permute-done.12 = f32[1,4,256]{2,0,1:T(1,128)S(1)} collective-permute-done((f32[1,4,256]{2,0,1:T(1,128)S(1)}, f32[1,4,256]{2,0,1:T(1,128)S(1)}, u32[]{:S(2)}, u32[]{:S(2)}) %collective-permute-start.12) | collective-permute-done | bytes 4128 | tf_op jit(solution)/shard_map/ppermute | solution.py:67
  127.0 5.7 %collective-permute-done.13 = f32[1,4,256]{2,0,1:T(1,128)S(1)} collective-permute-done((f32[1,4,256]{2,0,1:T(1,128)S(1)}, f32[1,4,256]{2,0,1:T(1,128)S(1)}, u32[]{:S(2)}, u32[]{:S(2)}) %collective-permute-start.13) | collective-permute-done | bytes 4128 | tf_op jit(solution)/shard_map/ppermute | solution.py:67
  132.8 5.7 %collective-permute-done.14 = f32[1,4,256]{2,0,1:T(1,128)S(1)} collective-permute-done((f32[1,4,256]{2,0,1:T(1,128)S(1)}, f32[1,4,256]{2,0,1:T(1,128)S(1)}, u32[]{:S(2)}, u32[]{:S(2)}) %collective-permute-start.14) | collective-permute-done | bytes 4128 | tf_op jit(solution)/shard_map/ppermute | solution.py:67
  152.6 5.7 %collective-permute-done.16 = f32[1,4,256]{2,0,1:T(1,128)S(1)} collective-permute-done((f32[1,4,256]{2,0,1:T(1,128)S(1)}, f32[1,4,256]{2,0,1:T(1,128)S(1)}, u32[]{:S(2)}, u32[]{:S(2)}) %collective-permute-start.16) | collective-permute-done | bytes 4128 | tf_op jit(solution)/shard_map/ppermute | solution.py:67
  158.3 5.7 %collective-permute-done.17 = f32[1,4,256]{2,0,1:T(1,128)S(1)} collective-permute-done((f32[1,4,256]{2,0,1:T(1,128)S(1)}, f32[1,4,256]{2,0,1:T(1,128)S(1)}, u32[]{:S(2)}, u32[]{:S(2)}) %collective-permute-start.17) | collective-permute-done | bytes 4128 | tf_op jit(solution)/shard_map/ppermute | solution.py:67
  164.1 5.7 %collective-permute-done.18 = f32[1,4,256]{2,0,1:T(1,128)S(1)} collective-permute-done((f32[1,4,256]{2,0,1:T(1,128)S(1)}, f32[1,4,256]{2,0,1:T(1,128)S(1)}, u32[]{:S(2)}, u32[]{:S(2)}) %collective-permute-start.18) | collective-permute-done | bytes 4128 | tf_op jit(solution)/shard_map/ppermute | solution.py:67
  169.8 5.7 %collective-permute-done.19 = f32[1,4,256]{2,0,1:T(1,128)S(1)} collective-permute-done((f32[1,4,256]{2,0,1:T(1,128)S(1)}, f32[1,4,256]{2,0,1:T(1,128)S(1)}, u32[]{:S(2)}, u32[]{:S(2)}) %collective-permute-start.19) | collective-permute-done | bytes 4128 | tf_op jit(solution)/shard_map/ppermute | solution.py:67
  175.5 5.7 %collective-permute-done.20 = f32[1,4,256]{2,0,1:T(1,128)S(1)} collective-permute-done((f32[1,4,256]{2,0,1:T(1,128)S(1)}, f32[1,4,256]{2,0,1:T(1,128)S(1)}, u32[]{:S(2)}, u32[]{:S(2)}) %collective-permute-start.20) | collective-permute-done | bytes 4128 | tf_op jit(solution)/shard_map/ppermute | solution.py:67
  181.2 5.7 %collective-permute-done.21 = f32[1,4,256]{2,0,1:T(1,128)S(1)} collective-permute-done((f32[1,4,256]{2,0,1:T(1,128)S(1)}, f32[1,4,256]{2,0,1:T(1,128)S(1)}, u32[]{:S(2)}, u32[]{:S(2)}) %collective-permute-start.21) | collective-permute-done | bytes 4128 | tf_op jit(solution)/shard_map/ppermute | solution.py:67
  187.0 5.7 %collective-permute-done.22 = f32[1,4,256]{2,0,1:T(1,128)S(1)} collective-permute-done((f32[1,4,256]{2,0,1:T(1,128)S(1)}, f32[1,4,256]{2,0,1:T(1,128)S(1)}, u32[]{:S(2)}, u32[]{:S(2)}) %collective-permute-start.22) | collective-permute-done | bytes 4128 | tf_op jit(solution)/shard_map/ppermute | solution.py:67
  192.7 5.7 %collective-permute-done.23 = f32[1,4,256]{2,0,1:T(1,128)S(1)} collective-permute-done((f32[1,4,256]{2,0,1:T(1,128)S(1)}, f32[1,4,256]{2,0,1:T(1,128)S(1)}, u32[]{:S(2)}, u32[]{:S(2)}) %collective-permute-start.23) | collective-permute-done | bytes 4128 | tf_op jit(solution)/shard_map/ppermute | solution.py:67
  198.4 5.7 %collective-permute-done.24 = f32[1,4,256]{2,0,1:T(1,128)S(1)} collective-permute-done((f32[1,4,256]{2,0,1:T(1,128)S(1)}, f32[1,4,256]{2,0,1:T(1,128)S(1)}, u32[]{:S(2)}, u32[]{:S(2)}) %collective-permute-start.24) | collective-permute-done | bytes 4128 | tf_op jit(solution)/shard_map/ppermute | solution.py:67
  204.2 5.7 %collective-permute-done.25 = f32[1,4,256]{2,0,1:T(1,128)S(1)} collective-permute-done((f32[1,4,256]{2,0,1:T(1,128)S(1)}, f32[1,4,256]{2,0,1:T(1,128)S(1)}, u32[]{:S(2)}, u32[]{:S(2)}) %collective-permute-start.25) | collective-permute-done | bytes 4128 | tf_op jit(solution)/shard_map/ppermute | solution.py:67
  209.9 5.7 %collective-permute-done.26 = f32[1,4,256]{2,0,1:T(1,128)S(1)} collective-permute-done((f32[1,4,256]{2,0,1:T(1,128)S(1)}, f32[1,4,256]{2,0,1:T(1,128)S(1)}, u32[]{:S(2)}, u32[]{:S(2)}) %collective-permute-start.26) | collective-permute-done | bytes 4128 | tf_op jit(solution)/shard_map/ppermute | solution.py:67
  215.6 5.7 %collective-permute-done.27 = f32[1,4,256]{2,0,1:T(1,128)S(1)} collective-permute-done((f32[1,4,256]{2,0,1:T(1,128)S(1)}, f32[1,4,256]{2,0,1:T(1,128)S(1)}, u32[]{:S(2)}, u32[]{:S(2)}) %collective-permute-start.27) | collective-permute-done | bytes 4128 | tf_op jit(solution)/shard_map/ppermute | solution.py:67
  221.4 5.7 %collective-permute-done.28 = f32[1,4,256]{2,0,1:T(1,128)S(1)} collective-permute-done((f32[1,4,256]{2,0,1:T(1,128)S(1)}, f32[1,4,256]{2,0,1:T(1,128)S(1)}, u32[]{:S(2)}, u32[]{:S(2)}) %collective-permute-start.28) | collective-permute-done | bytes 4128 | tf_op jit(solution)/shard_map/ppermute | solution.py:67
  250.5 34.4 %psum.7 = f32[4]{0:T(128)} all-reduce(f32[4]{0:T(128)S(1)} %broadcast_multiply_fusion), channel_id=1, replica_groups=mesh['groups'=2,'tm'=16] {'tm'}, use_global_device_ids=true, to_apply=%region_4.7 | all-reduce | flops 4 | bytes 32 | tf_op jit(solution)/shard_map/psum | solution.py:131
  284.9 5.7 %collective-permute-done.31 = f32[1,4,256]{2,0,1:T(1,128)S(1)} collective-permute-done((f32[1,4,256]{2,0,1:T(1,128)S(1)}, f32[1,4,256]{2,0,1:T(1,128)S(1)}, u32[]{:S(2)}, u32[]{:S(2)}) %collective-permute-start.31) | collective-permute-done | bytes 4128 | tf_op jit(solution)/shard_map/ppermute | solution.py:67
  290.7 5.7 %collective-permute-done.32 = f32[1,4,256]{2,0,1:T(1,128)S(1)} collective-permute-done((f32[1,4,256]{2,0,1:T(1,128)S(1)}, f32[1,4,256]{2,0,1:T(1,128)S(1)}, u32[]{:S(2)}, u32[]{:S(2)}) %collective-permute-start.32) | collective-permute-done | bytes 4128 | tf_op jit(solution)/shard_map/ppermute | solution.py:67
  296.4 5.7 %collective-permute-done.33 = f32[1,4,256]{2,0,1:T(1,128)S(1)} collective-permute-done((f32[1,4,256]{2,0,1:T(1,128)S(1)}, f32[1,4,256]{2,0,1:T(1,128)S(1)}, u32[]{:S(2)}, u32[]{:S(2)}) %collective-permute-start.33) | collective-permute-done | bytes 4128 | tf_op jit(solution)/shard_map/ppermute | solution.py:67
  302.1 5.7 %collective-permute-done.34 = f32[1,4,256]{2,0,1:T(1,128)S(1)} collective-permute-done((f32[1,4,256]{2,0,1:T(1,128)S(1)}, f32[1,4,256]{2,0,1:T(1,128)S(1)}, u32[]{:S(2)}, u32[]{:S(2)}) %collective-permute-start.34) | collective-permute-done | bytes 4128 | tf_op jit(solution)/shard_map/ppermute | solution.py:67
  307.8 5.7 %collective-permute-done.35 = f32[1,4,256]{2,0,1:T(1,128)S(1)} collective-permute-done((f32[1,4,256]{2,0,1:T(1,128)S(1)}, f32[1,4,256]{2,0,1:T(1,128)S(1)}, u32[]{:S(2)}, u32[]{:S(2)}) %collective-permute-start.35) | collective-permute-done | bytes 4128 | tf_op jit(solution)/shard_map/ppermute | solution.py:67
  313.6 5.7 %collective-permute-done.36 = f32[1,4,256]{2,0,1:T(1,128)S(1)} collective-permute-done((f32[1,4,256]{2,0,1:T(1,128)S(1)}, f32[1,4,256]{2,0,1:T(1,128)S(1)}, u32[]{:S(2)}, u32[]{:S(2)}) %collective-permute-start.36) | collective-permute-done | bytes 4128 | tf_op jit(solution)/shard_map/ppermute | solution.py:67
  319.3 5.7 %collective-permute-done.37 = f32[1,4,256]{2,0,1:T(1,128)S(1)} collective-permute-done((f32[1,4,256]{2,0,1:T(1,128)S(1)}, f32[1,4,256]{2,0,1:T(1,128)S(1)}, u32[]{:S(2)}, u32[]{:S(2)}) %collective-permute-start.37) | collective-permute-done | bytes 4128 | tf_op jit(solution)/shard_map/ppermute | solution.py:67
  325.0 5.7 %collective-permute-done.38 = f32[1,4,256]{2,0,1:T(1,128)S(1)} collective-permute-done((f32[1,4,256]{2,0,1:T(1,128)S(1)}, f32[1,4,256]{2,0,1:T(1,128)S(1)}, u32[]{:S(2)}, u32[]{:S(2)}) %collective-permute-start.38) | collective-permute-done | bytes 4128 | tf_op jit(solution)/shard_map/ppermute | solution.py:67
  330.8 5.7 %collective-permute-done.39 = f32[1,4,256]{2,0,1:T(1,128)S(1)} collective-permute-done((f32[1,4,256]{2,0,1:T(1,128)S(1)}, f32[1,4,256]{2,0,1:T(1,128)S(1)}, u32[]{:S(2)}, u32[]{:S(2)}) %collective-permute-start.39) | collective-permute-done | bytes 4128 | tf_op jit(solution)/shard_map/ppermute | solution.py:67
  336.5 5.7 %collective-permute-done.40 = f32[1,4,256]{2,0,1:T(1,128)S(1)} collective-permute-done((f32[1,4,256]{2,0,1:T(1,128)S(1)}, f32[1,4,256]{2,0,1:T(1,128)S(1)}, u32[]{:S(2)}, u32[]{:S(2)}) %collective-permute-start.40) | collective-permute-done | bytes 4128 | tf_op jit(solution)/shard_map/ppermute | solution.py:67
  342.2 5.7 %collective-permute-done.41 = f32[1,4,256]{2,0,1:T(1,128)S(1)} collective-permute-done((f32[1,4,256]{2,0,1:T(1,128)S(1)}, f32[1,4,256]{2,0,1:T(1,128)S(1)}, u32[]{:S(2)}, u32[]{:S(2)}) %collective-permute-start.41) | collective-permute-done | bytes 4128 | tf_op jit(solution)/shard_map/ppermute | solution.py:67
  348.0 5.7 %collective-permute-done.42 = f32[1,4,256]{2,0,1:T(1,128)S(1)} collective-permute-done((f32[1,4,256]{2,0,1:T(1,128)S(1)}, f32[1,4,256]{2,0,1:T(1,128)S(1)}, u32[]{:S(2)}, u32[]{:S(2)}) %collective-permute-start.42) | collective-permute-done | bytes 4128 | tf_op jit(solution)/shard_map/ppermute | solution.py:67
  353.7 5.7 %collective-permute-done.43 = f32[1,4,256]{2,0,1:T(1,128)S(1)} collective-permute-done((f32[1,4,256]{2,0,1:T(1,128)S(1)}, f32[1,4,256]{2,0,1:T(1,128)S(1)}, u32[]{:S(2)}, u32[]{:S(2)}) %collective-permute-start.43) | collective-permute-done | bytes 4128 | tf_op jit(solution)/shard_map/ppermute | solution.py:67
  359.4 5.7 %collective-permute-done.44 = f32[1,4,256]{2,0,1:T(1,128)S(1)} collective-permute-done((f32[1,4,256]{2,0,1:T(1,128)S(1)}, f32[1,4,256]{2,0,1:T(1,128)S(1)}, u32[]{:S(2)}, u32[]{:S(2)}) %collective-permute-start.44) | collective-permute-done | bytes 4128 | tf_op jit(solution)/shard_map/ppermute | solution.py:67
  389.9 5.7 %collective-permute-done.46 = f32[1,4,256]{2,0,1:T(1,128)S(1)} collective-permute-done((f32[1,4,256]{2,0,1:T(1,128)S(1)}, f32[1,4,256]{2,0,1:T(1,128)S(1)}, u32[]{:S(2)}, u32[]{:S(2)}) %collective-permute-start.46) | collective-permute-done | bytes 4128 | tf_op jit(solution)/shard_map/ppermute | solution.py:67
  395.6 5.7 %collective-permute-done.47 = f32[1,4,256]{2,0,1:T(1,128)S(1)} collective-permute-done((f32[1,4,256]{2,0,1:T(1,128)S(1)}, f32[1,4,256]{2,0,1:T(1,128)S(1)}, u32[]{:S(2)}, u32[]{:S(2)}) %collective-permute-start.47) | collective-permute-done | bytes 4128 | tf_op jit(solution)/shard_map/ppermute | solution.py:67
  401.3 5.7 %collective-permute-done.48 = f32[1,4,256]{2,0,1:T(1,128)S(1)} collective-permute-done((f32[1,4,256]{2,0,1:T(1,128)S(1)}, f32[1,4,256]{2,0,1:T(1,128)S(1)}, u32[]{:S(2)}, u32[]{:S(2)}) %collective-permute-start.48) | collective-permute-done | bytes 4128 | tf_op jit(solution)/shard_map/ppermute | solution.py:67
  407.1 5.7 %collective-permute-done.49 = f32[1,4,256]{2,0,1:T(1,128)S(1)} collective-permute-done((f32[1,4,256]{2,0,1:T(1,128)S(1)}, f32[1,4,256]{2,0,1:T(1,128)S(1)}, u32[]{:S(2)}, u32[]{:S(2)}) %collective-permute-start.49) | collective-permute-done | bytes 4128 | tf_op jit(solution)/shard_map/ppermute | solution.py:67
  412.8 5.7 %collective-permute-done.50 = f32[1,4,256]{2,0,1:T(1,128)S(1)} collective-permute-done((f32[1,4,256]{2,0,1:T(1,128)S(1)}, f32[1,4,256]{2,0,1:T(1,128)S(1)}, u32[]{:S(2)}, u32[]{:S(2)}) %collective-permute-start.50) | collective-permute-done | bytes 4128 | tf_op jit(solution)/shard_map/ppermute | solution.py:67
  (486 shorter events, 143.0 us)
Async XLA Ops:
  12.6 45.7 %collective-permute-start = (f32[1,4,256]{2,0,1:T(1,128)S(1)}, f32[1,4,256]{2,0,1:T(1,128)S(1)}, u32[]{:S(2)}, u32[]{:S(2)}) collective-permute-start(f32[1,4,256]{2,0,1:T(1,128)S(1)} %slice_bitcast_fusion.27), channel_id=1, source_target_pairs={{0,1},{1,2},{2,3},{3,4},{4,5},{5,6},{6,7},{7,8},{8,9},{9,10},{10,1... | collective-permute-start | bytes 12296 | tf_op jit(solution)/shard_map/ppermute | solution.py:67
  58.3 5.7 %collective-permute-start.1 = (f32[1,4,256]{2,0,1:T(1,128)S(1)}, f32[1,4,256]{2,0,1:T(1,128)S(1)}, u32[]{:S(2)}, u32[]{:S(2)}) collective-permute-start(f32[1,4,256]{2,0,1:T(1,128)S(1)} %collective-permute-done), channel_id=1, source_target_pairs={{0,1},{1,2},{2,3},{3,4},{4,5},{5,6},{6,7},{7,8},{8,9},{9,10},{10,1... | collective-permute-start | bytes 12296 | tf_op jit(solution)/shard_map/ppermute | solution.py:67
  64.0 5.7 %collective-permute-start.2 = (f32[1,4,256]{2,0,1:T(1,128)S(1)}, f32[1,4,256]{2,0,1:T(1,128)S(1)}, u32[]{:S(2)}, u32[]{:S(2)}) collective-permute-start(f32[1,4,256]{2,0,1:T(1,128)S(1)} %collective-permute-done.1), channel_id=1, source_target_pairs={{0,1},{1,2},{2,3},{3,4},{4,5},{5,6},{6,7},{7,8},{8,9},{9,10},{10,1... | collective-permute-start | bytes 12296 | tf_op jit(solution)/shard_map/ppermute | solution.py:67
  69.7 5.7 %collective-permute-start.3 = (f32[1,4,256]{2,0,1:T(1,128)S(1)}, f32[1,4,256]{2,0,1:T(1,128)S(1)}, u32[]{:S(2)}, u32[]{:S(2)}) collective-permute-start(f32[1,4,256]{2,0,1:T(1,128)S(1)} %collective-permute-done.2), channel_id=1, source_target_pairs={{0,1},{1,2},{2,3},{3,4},{4,5},{5,6},{6,7},{7,8},{8,9},{9,10},{10,1... | collective-permute-start | bytes 12296 | tf_op jit(solution)/shard_map/ppermute | solution.py:67
  75.5 5.7 %collective-permute-start.4 = (f32[1,4,256]{2,0,1:T(1,128)S(1)}, f32[1,4,256]{2,0,1:T(1,128)S(1)}, u32[]{:S(2)}, u32[]{:S(2)}) collective-permute-start(f32[1,4,256]{2,0,1:T(1,128)S(1)} %collective-permute-done.3), channel_id=1, source_target_pairs={{0,1},{1,2},{2,3},{3,4},{4,5},{5,6},{6,7},{7,8},{8,9},{9,10},{10,1... | collective-permute-start | bytes 12296 | tf_op jit(solution)/shard_map/ppermute | solution.py:67
  81.2 5.7 %collective-permute-start.5 = (f32[1,4,256]{2,0,1:T(1,128)S(1)}, f32[1,4,256]{2,0,1:T(1,128)S(1)}, u32[]{:S(2)}, u32[]{:S(2)}) collective-permute-start(f32[1,4,256]{2,0,1:T(1,128)S(1)} %collective-permute-done.4), channel_id=1, source_target_pairs={{0,1},{1,2},{2,3},{3,4},{4,5},{5,6},{6,7},{7,8},{8,9},{9,10},{10,1... | collective-permute-start | bytes 12296 | tf_op jit(solution)/shard_map/ppermute | solution.py:67
  86.9 5.7 %collective-permute-start.6 = (f32[1,4,256]{2,0,1:T(1,128)S(1)}, f32[1,4,256]{2,0,1:T(1,128)S(1)}, u32[]{:S(2)}, u32[]{:S(2)}) collective-permute-start(f32[1,4,256]{2,0,1:T(1,128)S(1)} %collective-permute-done.5), channel_id=1, source_target_pairs={{0,1},{1,2},{2,3},{3,4},{4,5},{5,6},{6,7},{7,8},{8,9},{9,10},{10,1... | collective-permute-start | bytes 12296 | tf_op jit(solution)/shard_map/ppermute | solution.py:67
  92.7 5.7 %collective-permute-start.7 = (f32[1,4,256]{2,0,1:T(1,128)S(1)}, f32[1,4,256]{2,0,1:T(1,128)S(1)}, u32[]{:S(2)}, u32[]{:S(2)}) collective-permute-start(f32[1,4,256]{2,0,1:T(1,128)S(1)} %collective-permute-done.6), channel_id=1, source_target_pairs={{0,1},{1,2},{2,3},{3,4},{4,5},{5,6},{6,7},{7,8},{8,9},{9,10},{10,1... | collective-permute-start | bytes 12296 | tf_op jit(solution)/shard_map/ppermute | solution.py:67
  98.4 5.7 %collective-permute-start.8 = (f32[1,4,256]{2,0,1:T(1,128)S(1)}, f32[1,4,256]{2,0,1:T(1,128)S(1)}, u32[]{:S(2)}, u32[]{:S(2)}) collective-permute-start(f32[1,4,256]{2,0,1:T(1,128)S(1)} %collective-permute-done.7), channel_id=1, source_target_pairs={{0,1},{1,2},{2,3},{3,4},{4,5},{5,6},{6,7},{7,8},{8,9},{9,10},{10,1... | collective-permute-start | bytes 12296 | tf_op jit(solution)/shard_map/ppermute | solution.py:67
  104.1 5.7 %collective-permute-start.9 = (f32[1,4,256]{2,0,1:T(1,128)S(1)}, f32[1,4,256]{2,0,1:T(1,128)S(1)}, u32[]{:S(2)}, u32[]{:S(2)}) collective-permute-start(f32[1,4,256]{2,0,1:T(1,128)S(1)} %collective-permute-done.8), channel_id=1, source_target_pairs={{0,1},{1,2},{2,3},{3,4},{4,5},{5,6},{6,7},{7,8},{8,9},{9,10},{10,1... | collective-permute-start | bytes 12296 | tf_op jit(solution)/shard_map/ppermute | solution.py:67
  109.8 5.7 %collective-permute-start.10 = (f32[1,4,256]{2,0,1:T(1,128)S(1)}, f32[1,4,256]{2,0,1:T(1,128)S(1)}, u32[]{:S(2)}, u32[]{:S(2)}) collective-permute-start(f32[1,4,256]{2,0,1:T(1,128)S(1)} %collective-permute-done.9), channel_id=1, source_target_pairs={{0,1},{1,2},{2,3},{3,4},{4,5},{5,6},{6,7},{7,8},{8,9},{9,10},{10,1... | collective-permute-start | bytes 12296 | tf_op jit(solution)/shard_map/ppermute | solution.py:67
  115.6 5.7 %collective-permute-start.11 = (f32[1,4,256]{2,0,1:T(1,128)S(1)}, f32[1,4,256]{2,0,1:T(1,128)S(1)}, u32[]{:S(2)}, u32[]{:S(2)}) collective-permute-start(f32[1,4,256]{2,0,1:T(1,128)S(1)} %collective-permute-done.10), channel_id=1, source_target_pairs={{0,1},{1,2},{2,3},{3,4},{4,5},{5,6},{6,7},{7,8},{8,9},{9,10},{10,1... | collective-permute-start | bytes 12296 | tf_op jit(solution)/shard_map/ppermute | solution.py:67
  121.3 5.7 %collective-permute-start.12 = (f32[1,4,256]{2,0,1:T(1,128)S(1)}, f32[1,4,256]{2,0,1:T(1,128)S(1)}, u32[]{:S(2)}, u32[]{:S(2)}) collective-permute-start(f32[1,4,256]{2,0,1:T(1,128)S(1)} %collective-permute-done.11), channel_id=1, source_target_pairs={{0,1},{1,2},{2,3},{3,4},{4,5},{5,6},{6,7},{7,8},{8,9},{9,10},{10,1... | collective-permute-start | bytes 12296 | tf_op jit(solution)/shard_map/ppermute | solution.py:67
  127.0 5.7 %collective-permute-start.13 = (f32[1,4,256]{2,0,1:T(1,128)S(1)}, f32[1,4,256]{2,0,1:T(1,128)S(1)}, u32[]{:S(2)}, u32[]{:S(2)}) collective-permute-start(f32[1,4,256]{2,0,1:T(1,128)S(1)} %collective-permute-done.12), channel_id=1, source_target_pairs={{0,1},{1,2},{2,3},{3,4},{4,5},{5,6},{6,7},{7,8},{8,9},{9,10},{10,1... | collective-permute-start | bytes 12296 | tf_op jit(solution)/shard_map/ppermute | solution.py:67
  132.8 5.7 %collective-permute-start.14 = (f32[1,4,256]{2,0,1:T(1,128)S(1)}, f32[1,4,256]{2,0,1:T(1,128)S(1)}, u32[]{:S(2)}, u32[]{:S(2)}) collective-permute-start(f32[1,4,256]{2,0,1:T(1,128)S(1)} %collective-permute-done.13), channel_id=1, source_target_pairs={{0,1},{1,2},{2,3},{3,4},{4,5},{5,6},{6,7},{7,8},{8,9},{9,10},{10,1... | collective-permute-start | bytes 12296 | tf_op jit(solution)/shard_map/ppermute | solution.py:67
  146.8 5.8 %collective-permute-start.15 = (f32[1,4,256]{2,0,1:T(1,128)S(1)}, f32[1,4,256]{2,0,1:T(1,128)S(1)}, u32[]{:S(2)}, u32[]{:S(2)}) collective-permute-start(f32[1,4,256]{2,0,1:T(1,128)S(1)} %slice_bitcast_fusion.23), channel_id=1, source_target_pairs={{0,1},{1,2},{2,3},{3,4},{4,5},{5,6},{6,7},{7,8},{8,9},{9,10},{10,1... | collective-permute-start | bytes 12296 | tf_op jit(solution)/shard_map/ppermute | solution.py:67
  152.6 5.7 %collective-permute-start.16 = (f32[1,4,256]{2,0,1:T(1,128)S(1)}, f32[1,4,256]{2,0,1:T(1,128)S(1)}, u32[]{:S(2)}, u32[]{:S(2)}) collective-permute-start(f32[1,4,256]{2,0,1:T(1,128)S(1)} %collective-permute-done.15), channel_id=1, source_target_pairs={{0,1},{1,2},{2,3},{3,4},{4,5},{5,6},{6,7},{7,8},{8,9},{9,10},{10,1... | collective-permute-start | bytes 12296 | tf_op jit(solution)/shard_map/ppermute | solution.py:67
  158.3 5.7 %collective-permute-start.17 = (f32[1,4,256]{2,0,1:T(1,128)S(1)}, f32[1,4,256]{2,0,1:T(1,128)S(1)}, u32[]{:S(2)}, u32[]{:S(2)}) collective-permute-start(f32[1,4,256]{2,0,1:T(1,128)S(1)} %collective-permute-done.16), channel_id=1, source_target_pairs={{0,1},{1,2},{2,3},{3,4},{4,5},{5,6},{6,7},{7,8},{8,9},{9,10},{10,1... | collective-permute-start | bytes 12296 | tf_op jit(solution)/shard_map/ppermute | solution.py:67
  164.0 5.7 %collective-permute-start.18 = (f32[1,4,256]{2,0,1:T(1,128)S(1)}, f32[1,4,256]{2,0,1:T(1,128)S(1)}, u32[]{:S(2)}, u32[]{:S(2)}) collective-permute-start(f32[1,4,256]{2,0,1:T(1,128)S(1)} %collective-permute-done.17), channel_id=1, source_target_pairs={{0,1},{1,2},{2,3},{3,4},{4,5},{5,6},{6,7},{7,8},{8,9},{9,10},{10,1... | collective-permute-start | bytes 12296 | tf_op jit(solution)/shard_map/ppermute | solution.py:67
  169.8 5.7 %collective-permute-start.19 = (f32[1,4,256]{2,0,1:T(1,128)S(1)}, f32[1,4,256]{2,0,1:T(1,128)S(1)}, u32[]{:S(2)}, u32[]{:S(2)}) collective-permute-start(f32[1,4,256]{2,0,1:T(1,128)S(1)} %collective-permute-done.18), channel_id=1, source_target_pairs={{0,1},{1,2},{2,3},{3,4},{4,5},{5,6},{6,7},{7,8},{8,9},{9,10},{10,1... | collective-permute-start | bytes 12296 | tf_op jit(solution)/shard_map/ppermute | solution.py:67
  175.5 5.7 %collective-permute-start.20 = (f32[1,4,256]{2,0,1:T(1,128)S(1)}, f32[1,4,256]{2,0,1:T(1,128)S(1)}, u32[]{:S(2)}, u32[]{:S(2)}) collective-permute-start(f32[1,4,256]{2,0,1:T(1,128)S(1)} %collective-permute-done.19), channel_id=1, source_target_pairs={{0,1},{1,2},{2,3},{3,4},{4,5},{5,6},{6,7},{7,8},{8,9},{9,10},{10,1... | collective-permute-start | bytes 12296 | tf_op jit(solution)/shard_map/ppermute | solution.py:67
  181.2 5.7 %collective-permute-start.21 = (f32[1,4,256]{2,0,1:T(1,128)S(1)}, f32[1,4,256]{2,0,1:T(1,128)S(1)}, u32[]{:S(2)}, u32[]{:S(2)}) collective-permute-start(f32[1,4,256]{2,0,1:T(1,128)S(1)} %collective-permute-done.20), channel_id=1, source_target_pairs={{0,1},{1,2},{2,3},{3,4},{4,5},{5,6},{6,7},{7,8},{8,9},{9,10},{10,1... | collective-permute-start | bytes 12296 | tf_op jit(solution)/shard_map/ppermute | solution.py:67
  187.0 5.7 %collective-permute-start.22 = (f32[1,4,256]{2,0,1:T(1,128)S(1)}, f32[1,4,256]{2,0,1:T(1,128)S(1)}, u32[]{:S(2)}, u32[]{:S(2)}) collective-permute-start(f32[1,4,256]{2,0,1:T(1,128)S(1)} %collective-permute-done.21), channel_id=1, source_target_pairs={{0,1},{1,2},{2,3},{3,4},{4,5},{5,6},{6,7},{7,8},{8,9},{9,10},{10,1... | collective-permute-start | bytes 12296 | tf_op jit(solution)/shard_map/ppermute | solution.py:67
  192.7 5.7 %collective-permute-start.23 = (f32[1,4,256]{2,0,1:T(1,128)S(1)}, f32[1,4,256]{2,0,1:T(1,128)S(1)}, u32[]{:S(2)}, u32[]{:S(2)}) collective-permute-start(f32[1,4,256]{2,0,1:T(1,128)S(1)} %collective-permute-done.22), channel_id=1, source_target_pairs={{0,1},{1,2},{2,3},{3,4},{4,5},{5,6},{6,7},{7,8},{8,9},{9,10},{10,1... | collective-permute-start | bytes 12296 | tf_op jit(solution)/shard_map/ppermute | solution.py:67
  198.4 5.7 %collective-permute-start.24 = (f32[1,4,256]{2,0,1:T(1,128)S(1)}, f32[1,4,256]{2,0,1:T(1,128)S(1)}, u32[]{:S(2)}, u32[]{:S(2)}) collective-permute-start(f32[1,4,256]{2,0,1:T(1,128)S(1)} %collective-permute-done.23), channel_id=1, source_target_pairs={{0,1},{1,2},{2,3},{3,4},{4,5},{5,6},{6,7},{7,8},{8,9},{9,10},{10,1... | collective-permute-start | bytes 12296 | tf_op jit(solution)/shard_map/ppermute | solution.py:67
  204.2 5.7 %collective-permute-start.25 = (f32[1,4,256]{2,0,1:T(1,128)S(1)}, f32[1,4,256]{2,0,1:T(1,128)S(1)}, u32[]{:S(2)}, u32[]{:S(2)}) collective-permute-start(f32[1,4,256]{2,0,1:T(1,128)S(1)} %collective-permute-done.24), channel_id=1, source_target_pairs={{0,1},{1,2},{2,3},{3,4},{4,5},{5,6},{6,7},{7,8},{8,9},{9,10},{10,1... | collective-permute-start | bytes 12296 | tf_op jit(solution)/shard_map/ppermute | solution.py:67
  209.9 5.7 %collective-permute-start.26 = (f32[1,4,256]{2,0,1:T(1,128)S(1)}, f32[1,4,256]{2,0,1:T(1,128)S(1)}, u32[]{:S(2)}, u32[]{:S(2)}) collective-permute-start(f32[1,4,256]{2,0,1:T(1,128)S(1)} %collective-permute-done.25), channel_id=1, source_target_pairs={{0,1},{1,2},{2,3},{3,4},{4,5},{5,6},{6,7},{7,8},{8,9},{9,10},{10,1... | collective-permute-start | bytes 12296 | tf_op jit(solution)/shard_map/ppermute | solution.py:67
  215.6 5.7 %collective-permute-start.27 = (f32[1,4,256]{2,0,1:T(1,128)S(1)}, f32[1,4,256]{2,0,1:T(1,128)S(1)}, u32[]{:S(2)}, u32[]{:S(2)}) collective-permute-start(f32[1,4,256]{2,0,1:T(1,128)S(1)} %collective-permute-done.26), channel_id=1, source_target_pairs={{0,1},{1,2},{2,3},{3,4},{4,5},{5,6},{6,7},{7,8},{8,9},{9,10},{10,1... | collective-permute-start | bytes 12296 | tf_op jit(solution)/shard_map/ppermute | solution.py:67
  221.3 5.7 %collective-permute-start.28 = (f32[1,4,256]{2,0,1:T(1,128)S(1)}, f32[1,4,256]{2,0,1:T(1,128)S(1)}, u32[]{:S(2)}, u32[]{:S(2)}) collective-permute-start(f32[1,4,256]{2,0,1:T(1,128)S(1)} %collective-permute-done.27), channel_id=1, source_target_pairs={{0,1},{1,2},{2,3},{3,4},{4,5},{5,6},{6,7},{7,8},{8,9},{9,10},{10,1... | collective-permute-start | bytes 12296 | tf_op jit(solution)/shard_map/ppermute | solution.py:67
  227.1 5.7 %collective-permute-start.29 = (f32[1,4,256]{2,0,1:T(1,128)S(1)}, f32[1,4,256]{2,0,1:T(1,128)S(1)}, u32[]{:S(2)}, u32[]{:S(2)}) collective-permute-start(f32[1,4,256]{2,0,1:T(1,128)S(1)} %collective-permute-done.28), channel_id=1, source_target_pairs={{0,1},{1,2},{2,3},{3,4},{4,5},{5,6},{6,7},{7,8},{8,9},{9,10},{10,1... | collective-permute-start | bytes 12296 | tf_op jit(solution)/shard_map/ppermute | solution.py:67
  250.4 34.5 %collective-permute-start.30 = (f32[1,4,256]{2,0,1:T(1,128)S(1)}, f32[1,4,256]{2,0,1:T(1,128)S(1)}, u32[]{:S(2)}, u32[]{:S(2)}) collective-permute-start(f32[1,4,256]{2,0,1:T(1,128)S(1)} %slice_bitcast_fusion.19), channel_id=1, source_target_pairs={{0,1},{1,2},{2,3},{3,4},{4,5},{5,6},{6,7},{7,8},{8,9},{9,10},{10,1... | collective-permute-start | bytes 12296 | tf_op jit(solution)/shard_map/ppermute | solution.py:67
  284.9 5.7 %collective-permute-start.31 = (f32[1,4,256]{2,0,1:T(1,128)S(1)}, f32[1,4,256]{2,0,1:T(1,128)S(1)}, u32[]{:S(2)}, u32[]{:S(2)}) collective-permute-start(f32[1,4,256]{2,0,1:T(1,128)S(1)} %collective-permute-done.30), channel_id=1, source_target_pairs={{0,1},{1,2},{2,3},{3,4},{4,5},{5,6},{6,7},{7,8},{8,9},{9,10},{10,1... | collective-permute-start | bytes 12296 | tf_op jit(solution)/shard_map/ppermute | solution.py:67
  290.6 5.7 %collective-permute-start.32 = (f32[1,4,256]{2,0,1:T(1,128)S(1)}, f32[1,4,256]{2,0,1:T(1,128)S(1)}, u32[]{:S(2)}, u32[]{:S(2)}) collective-permute-start(f32[1,4,256]{2,0,1:T(1,128)S(1)} %collective-permute-done.31), channel_id=1, source_target_pairs={{0,1},{1,2},{2,3},{3,4},{4,5},{5,6},{6,7},{7,8},{8,9},{9,10},{10,1... | collective-permute-start | bytes 12296 | tf_op jit(solution)/shard_map/ppermute | solution.py:67
  296.4 5.7 %collective-permute-start.33 = (f32[1,4,256]{2,0,1:T(1,128)S(1)}, f32[1,4,256]{2,0,1:T(1,128)S(1)}, u32[]{:S(2)}, u32[]{:S(2)}) collective-permute-start(f32[1,4,256]{2,0,1:T(1,128)S(1)} %collective-permute-done.32), channel_id=1, source_target_pairs={{0,1},{1,2},{2,3},{3,4},{4,5},{5,6},{6,7},{7,8},{8,9},{9,10},{10,1... | collective-permute-start | bytes 12296 | tf_op jit(solution)/shard_map/ppermute | solution.py:67
  302.1 5.7 %collective-permute-start.34 = (f32[1,4,256]{2,0,1:T(1,128)S(1)}, f32[1,4,256]{2,0,1:T(1,128)S(1)}, u32[]{:S(2)}, u32[]{:S(2)}) collective-permute-start(f32[1,4,256]{2,0,1:T(1,128)S(1)} %collective-permute-done.33), channel_id=1, source_target_pairs={{0,1},{1,2},{2,3},{3,4},{4,5},{5,6},{6,7},{7,8},{8,9},{9,10},{10,1... | collective-permute-start | bytes 12296 | tf_op jit(solution)/shard_map/ppermute | solution.py:67
  307.8 5.7 %collective-permute-start.35 = (f32[1,4,256]{2,0,1:T(1,128)S(1)}, f32[1,4,256]{2,0,1:T(1,128)S(1)}, u32[]{:S(2)}, u32[]{:S(2)}) collective-permute-start(f32[1,4,256]{2,0,1:T(1,128)S(1)} %collective-permute-done.34), channel_id=1, source_target_pairs={{0,1},{1,2},{2,3},{3,4},{4,5},{5,6},{6,7},{7,8},{8,9},{9,10},{10,1... | collective-permute-start | bytes 12296 | tf_op jit(solution)/shard_map/ppermute | solution.py:67
  313.6 5.7 %collective-permute-start.36 = (f32[1,4,256]{2,0,1:T(1,128)S(1)}, f32[1,4,256]{2,0,1:T(1,128)S(1)}, u32[]{:S(2)}, u32[]{:S(2)}) collective-permute-start(f32[1,4,256]{2,0,1:T(1,128)S(1)} %collective-permute-done.35), channel_id=1, source_target_pairs={{0,1},{1,2},{2,3},{3,4},{4,5},{5,6},{6,7},{7,8},{8,9},{9,10},{10,1... | collective-permute-start | bytes 12296 | tf_op jit(solution)/shard_map/ppermute | solution.py:67
  319.3 5.7 %collective-permute-start.37 = (f32[1,4,256]{2,0,1:T(1,128)S(1)}, f32[1,4,256]{2,0,1:T(1,128)S(1)}, u32[]{:S(2)}, u32[]{:S(2)}) collective-permute-start(f32[1,4,256]{2,0,1:T(1,128)S(1)} %collective-permute-done.36), channel_id=1, source_target_pairs={{0,1},{1,2},{2,3},{3,4},{4,5},{5,6},{6,7},{7,8},{8,9},{9,10},{10,1... | collective-permute-start | bytes 12296 | tf_op jit(solution)/shard_map/ppermute | solution.py:67
  325.0 5.7 %collective-permute-start.38 = (f32[1,4,256]{2,0,1:T(1,128)S(1)}, f32[1,4,256]{2,0,1:T(1,128)S(1)}, u32[]{:S(2)}, u32[]{:S(2)}) collective-permute-start(f32[1,4,256]{2,0,1:T(1,128)S(1)} %collective-permute-done.37), channel_id=1, source_target_pairs={{0,1},{1,2},{2,3},{3,4},{4,5},{5,6},{6,7},{7,8},{8,9},{9,10},{10,1... | collective-permute-start | bytes 12296 | tf_op jit(solution)/shard_map/ppermute | solution.py:67
  330.8 5.7 %collective-permute-start.39 = (f32[1,4,256]{2,0,1:T(1,128)S(1)}, f32[1,4,256]{2,0,1:T(1,128)S(1)}, u32[]{:S(2)}, u32[]{:S(2)}) collective-permute-start(f32[1,4,256]{2,0,1:T(1,128)S(1)} %collective-permute-done.38), channel_id=1, source_target_pairs={{0,1},{1,2},{2,3},{3,4},{4,5},{5,6},{6,7},{7,8},{8,9},{9,10},{10,1... | collective-permute-start | bytes 12296 | tf_op jit(solution)/shard_map/ppermute | solution.py:67
  336.5 5.7 %collective-permute-start.40 = (f32[1,4,256]{2,0,1:T(1,128)S(1)}, f32[1,4,256]{2,0,1:T(1,128)S(1)}, u32[]{:S(2)}, u32[]{:S(2)}) collective-permute-start(f32[1,4,256]{2,0,1:T(1,128)S(1)} %collective-permute-done.39), channel_id=1, source_target_pairs={{0,1},{1,2},{2,3},{3,4},{4,5},{5,6},{6,7},{7,8},{8,9},{9,10},{10,1... | collective-permute-start | bytes 12296 | tf_op jit(solution)/shard_map/ppermute | solution.py:67
  342.2 5.7 %collective-permute-start.41 = (f32[1,4,256]{2,0,1:T(1,128)S(1)}, f32[1,4,256]{2,0,1:T(1,128)S(1)}, u32[]{:S(2)}, u32[]{:S(2)}) collective-permute-start(f32[1,4,256]{2,0,1:T(1,128)S(1)} %collective-permute-done.40), channel_id=1, source_target_pairs={{0,1},{1,2},{2,3},{3,4},{4,5},{5,6},{6,7},{7,8},{8,9},{9,10},{10,1... | collective-permute-start | bytes 12296 | tf_op jit(solution)/shard_map/ppermute | solution.py:67
  347.9 5.7 %collective-permute-start.42 = (f32[1,4,256]{2,0,1:T(1,128)S(1)}, f32[1,4,256]{2,0,1:T(1,128)S(1)}, u32[]{:S(2)}, u32[]{:S(2)}) collective-permute-start(f32[1,4,256]{2,0,1:T(1,128)S(1)} %collective-permute-done.41), channel_id=1, source_target_pairs={{0,1},{1,2},{2,3},{3,4},{4,5},{5,6},{6,7},{7,8},{8,9},{9,10},{10,1... | collective-permute-start | bytes 12296 | tf_op jit(solution)/shard_map/ppermute | solution.py:67
  353.7 5.7 %collective-permute-start.43 = (f32[1,4,256]{2,0,1:T(1,128)S(1)}, f32[1,4,256]{2,0,1:T(1,128)S(1)}, u32[]{:S(2)}, u32[]{:S(2)}) collective-permute-start(f32[1,4,256]{2,0,1:T(1,128)S(1)} %collective-permute-done.42), channel_id=1, source_target_pairs={{0,1},{1,2},{2,3},{3,4},{4,5},{5,6},{6,7},{7,8},{8,9},{9,10},{10,1... | collective-permute-start | bytes 12296 | tf_op jit(solution)/shard_map/ppermute | solution.py:67
  359.4 5.7 %collective-permute-start.44 = (f32[1,4,256]{2,0,1:T(1,128)S(1)}, f32[1,4,256]{2,0,1:T(1,128)S(1)}, u32[]{:S(2)}, u32[]{:S(2)}) collective-permute-start(f32[1,4,256]{2,0,1:T(1,128)S(1)} %collective-permute-done.43), channel_id=1, source_target_pairs={{0,1},{1,2},{2,3},{3,4},{4,5},{5,6},{6,7},{7,8},{8,9},{9,10},{10,1... | collective-permute-start | bytes 12296 | tf_op jit(solution)/shard_map/ppermute | solution.py:67
  384.1 5.8 %collective-permute-start.45 = (f32[1,4,256]{2,0,1:T(1,128)S(1)}, f32[1,4,256]{2,0,1:T(1,128)S(1)}, u32[]{:S(2)}, u32[]{:S(2)}) collective-permute-start(f32[1,4,256]{2,0,1:T(1,128)S(1)} %slice_bitcast_fusion.15), channel_id=1, source_target_pairs={{0,1},{1,2},{2,3},{3,4},{4,5},{5,6},{6,7},{7,8},{8,9},{9,10},{10,1... | collective-permute-start | bytes 12296 | tf_op jit(solution)/shard_map/ppermute | solution.py:67
  389.9 5.7 %collective-permute-start.46 = (f32[1,4,256]{2,0,1:T(1,128)S(1)}, f32[1,4,256]{2,0,1:T(1,128)S(1)}, u32[]{:S(2)}, u32[]{:S(2)}) collective-permute-start(f32[1,4,256]{2,0,1:T(1,128)S(1)} %collective-permute-done.45), channel_id=1, source_target_pairs={{0,1},{1,2},{2,3},{3,4},{4,5},{5,6},{6,7},{7,8},{8,9},{9,10},{10,1... | collective-permute-start | bytes 12296 | tf_op jit(solution)/shard_map/ppermute | solution.py:67
  395.6 5.7 %collective-permute-start.47 = (f32[1,4,256]{2,0,1:T(1,128)S(1)}, f32[1,4,256]{2,0,1:T(1,128)S(1)}, u32[]{:S(2)}, u32[]{:S(2)}) collective-permute-start(f32[1,4,256]{2,0,1:T(1,128)S(1)} %collective-permute-done.46), channel_id=1, source_target_pairs={{0,1},{1,2},{2,3},{3,4},{4,5},{5,6},{6,7},{7,8},{8,9},{9,10},{10,1... | collective-permute-start | bytes 12296 | tf_op jit(solution)/shard_map/ppermute | solution.py:67
  (76 other events, 1643.9 us)
